TPU v7x, 32 devices: a whole 2x2x4 slice. The times are simulated.
32 devices in a mesh: group: 2 (over y), seq: 8 (over z, x), head: 2 (over core).
Axes of the slice: x: 2, y: 2, z: 4, core: 2. Of those that a mesh axis runs over, the one named last changes fastest.
Arguments:
- x_in: bfloat16 [4096, 4096], P(('group', 'seq'), 'head'), parts along dimension 0, may hold values from -6 to 6
- step_size: float32 [64, 4096], P('head', ('group', 'seq')), parts along dimension 1, may hold values from 0.002 to 0.128
- a_log: float32 [64], P('head'), may hold values from -8.5 to 0.9
- d_skip: float32 [64], P('head'), may hold values from 0.1 to 1.9
- b_in: bfloat16 [4096, 128], P(('group', 'seq')), parts along dimension 0, may hold values from -6 to 6
- c_in: bfloat16 [4096, 128], P(('group', 'seq')), parts along dimension 0, may hold values from -0.52734375 to 0.52734375
- queries: bfloat16 [4096, 2048], P(('group', 'seq'), 'head'), parts along dimension 0, may hold values from -4.5 to 4.5
- key_rows: bfloat16 [4096, 512], P(('group', 'seq'), 'head'), parts along dimension 0, may hold values from -4.5 to 4.5
- values: bfloat16 [4096, 512], P(('group', 'seq'), 'head'), parts along dimension 0, may hold values from -6 to 6
Outputs:
- mamba_out: bfloat16 [4096, 4096], P(('group', 'seq'), 'head'), parts along dimension 0
- attn_out: bfloat16 [4096, 2048], P(('group', 'seq'), 'head'), parts along dimension 0
There are 2 independent parts, one for each index of `group`. A program takes and returns all parts, laid end to end along the dimension named above; an argument that names none is the same for every part. Nothing has to cross between parts.
All inputs are finite; a program needn't handle non-finite values.
Results may differ from a plain program's by a relative error of at most 0.009.
Values may be sent and summed in bfloat16 or wider, within the bound.
No kernel may reach another device: no remote copies, remote signals or barrier semaphores. Data moves between devices by JAX's collectives and lax.ppermute only.
A program may use at most 320 MiB of HBM per device.

v0:
```python
import jax
import jax.numpy as jnp
from jax import lax
from jax.sharding import PartitionSpec as P

BLOCK = 128
HEADDIM = 64
STATE = 128
QHEADS = 16
KVHEADS = 4
HD = 128
NEG = -1e30


def carried_in(value, axis, combine, identity):
    count, mine = (lax.axis_size(axis), lax.axis_index(axis))
    everything = jax.tree.map(
        lambda part, kind: lax.all_gather(part.astype(kind), axis),
        value,
        (jnp.bfloat16, jnp.bfloat16),
    )
    start = jax.tree.map(
        lambda part, zero: jnp.broadcast_to(jnp.asarray(zero, part.dtype), part.shape),
        value,
        identity,
    )

    def turn(k, before):
        reached = k < mine
        new = combine(
            before, jax.tree.map(lambda part, own: part[k].astype(own.dtype), everything, value)
        )
        return jax.tree.map(lambda a, b: jnp.where(reached, a, b), new, before)

    return lax.fori_loop(0, count, turn, start)


def broadcast(value, axis, source):
    kept = jnp.where(lax.axis_index(axis) == source, value, 0).astype(value.dtype)
    return lax.psum(kept, axis)


def ssd_local(x_blocks, steps, rate, b_blocks, c_blocks):
    cum = jnp.cumsum(steps * rate[None, :, None], axis=2)
    causal = jnp.arange(BLOCK)[:, None] >= jnp.arange(BLOCK)[None, :]
    log_gap = jnp.where(causal, cum[:, :, :, None] - cum[:, :, None, :], -jnp.inf)
    inner = jnp.einsum("cin,cjn->cij", c_blocks, b_blocks, preferred_element_type=jnp.float32)
    mixing = (inner[:, None] * jnp.exp(log_gap) * steps[:, :, None, :]).astype(jnp.bfloat16)
    intra = jnp.einsum("chij,cjhp->cihp", mixing, x_blocks, preferred_element_type=jnp.float32)
    log_total = cum[:, :, -1]
    factor = (jnp.exp(log_total[:, :, None] - cum) * steps).transpose(0, 2, 1)[..., None]
    scaled = (factor * x_blocks.astype(jnp.float32)).astype(jnp.bfloat16)
    block_state = jnp.einsum("cjhp,cjn->chpn", scaled, b_blocks, preferred_element_type=jnp.float32)
    return (intra, block_state, log_total, cum)


def ssd_finish(intra, cum, c_blocks, incoming, d_skip, x_blocks):
    carried = jnp.einsum(
        "cin,chpn->cihp", c_blocks.astype(jnp.float32), incoming, precision=lax.Precision.HIGHEST
    )
    carried = carried * jnp.exp(cum).transpose(0, 2, 1)[..., None]
    return (intra + carried + d_skip[None, None, :, None] * x_blocks.astype(jnp.float32)).astype(
        jnp.bfloat16
    )


def chain(earlier, later):
    return (earlier[0] * later[0], later[0][..., None, None] * earlier[1] + later[1])


def local(x_in, step_size, a_log, d_skip, b_in, c_in, queries, key_rows, values):
    my_index = lax.axis_index("seq")
    seq_count = lax.axis_size("seq")
    tok_rows = x_in.shape[0]
    slots = tok_rows // BLOCK
    mamba_local = step_size.shape[0]
    rate = -jnp.exp(a_log)
    x_blocks = x_in.reshape(slots, BLOCK, mamba_local, HEADDIM)
    steps = step_size.reshape(mamba_local, slots, BLOCK).transpose(1, 0, 2)
    b_blocks = b_in.reshape(slots, BLOCK, STATE)
    c_blocks = c_in.reshape(slots, BLOCK, STATE)
    intra, block_state, log_total, cum = ssd_local(x_blocks, steps, rate, b_blocks, c_blocks)
    decay = jnp.exp(log_total)
    identity = (jnp.ones_like(decay), jnp.zeros_like(block_state))
    prefix = carried_in((decay, block_state), "seq", chain, identity)
    inclusive = chain(prefix, (decay, block_state))
    total_decay, total_state = (
        broadcast(inclusive[0].astype(jnp.bfloat16), "seq", lax.axis_size("seq") - 1).astype(
            jnp.float32
        ),
        broadcast(inclusive[1].astype(jnp.bfloat16), "seq", lax.axis_size("seq") - 1).astype(
            jnp.float32
        ),
    )
    carry_state = jnp.zeros_like(block_state[0])
    entering = []
    for slot in range(slots):
        entering.append(prefix[0][slot][:, None, None] * carry_state + prefix[1][slot])
        carry_state = total_decay[slot][:, None, None] * carry_state + total_state[slot]
    incoming = jnp.stack(entering, axis=0)
    mamba_out = ssd_finish(intra, cum, c_blocks, incoming, d_skip, x_blocks).reshape(
        tok_rows, mamba_local * HEADDIM
    )
    per_kv = QHEADS // KVHEADS
    kv_local = key_rows.shape[1] // HD
    score_scale = 1.0 / HD**0.5
    stride = seq_count * BLOCK
    q_flat = queries.reshape(slots, BLOCK, kv_local, per_kv, HD).transpose(2, 0, 3, 1, 4)
    q_flat = q_flat.reshape(kv_local, slots * per_kv * BLOCK, HD)
    q_slot = jnp.arange(slots)[:, None, None]
    q_row = jnp.arange(BLOCK)[None, None, :]
    query_pos = (
        q_slot * stride + my_index * BLOCK + q_row + jnp.zeros((slots, per_kv, BLOCK), jnp.int32)
    ).reshape(-1)
    k_slots = key_rows.reshape(slots, BLOCK, kv_local * HD)
    v_slots = values.reshape(slots, BLOCK, kv_local * HD)
    q_total = slots * per_kv * BLOCK
    start_state = (
        jnp.full((kv_local, q_total), NEG, jnp.float32),
        jnp.zeros((kv_local, q_total), jnp.float32),
        jnp.zeros((kv_local, q_total, HD), jnp.float32),
    )
    running = start_state
    k_piece = lax.all_gather(k_slots, "seq", axis=1, tiled=True)
    v_piece = lax.all_gather(v_slots, "seq", axis=1, tiled=True)
    rows = k_piece.shape[1]
    block_rows = 512
    count = rows // block_rows
    k_blocks = k_piece.reshape(slots, count, block_rows, kv_local, HD).transpose(1, 0, 2, 3, 4)
    v_blocks = v_piece.reshape(slots, count, block_rows, kv_local, HD).transpose(1, 0, 2, 3, 4)
    k_slot = jnp.arange(slots)[:, None]
    k_row = jnp.arange(block_rows)[None, :]

    def per_block(state, inputs):
        k_block, v_block, number = inputs
        run_max, run_sum, run_acc = state
        k_flat = k_block.reshape(slots * block_rows, kv_local, HD)
        v_flat = v_block.reshape(slots * block_rows, kv_local, HD)
        key_pos = (k_slot * stride + number * block_rows + k_row).reshape(-1)
        visible = key_pos[None, None, :] <= query_pos[None, :, None]
        scores = (
            jnp.einsum("gqd,kgd->gqk", q_flat, k_flat, preferred_element_type=jnp.float32)
            * score_scale
        )
        scores = jnp.where(visible, scores, NEG)
        new_max = jnp.maximum(run_max, jnp.max(scores, axis=-1))
        rescale = jnp.exp(run_max - new_max)
        weights = jnp.where(visible, jnp.exp(scores - new_max[..., None]), 0.0)
        new_sum = run_sum * rescale + jnp.sum(weights, axis=-1)
        update = jnp.einsum(
            "gqk,kgd->gqd", weights.astype(jnp.bfloat16), v_flat, preferred_element_type=jnp.float32
        )
        return ((new_max, new_sum, run_acc * rescale[..., None] + update), None)

    numbers = jnp.arange(count)
    running, unused = lax.scan(per_block, running, (k_blocks, v_blocks, numbers))
    run_max, run_sum, run_acc = running
    attended = (run_acc / run_sum[..., None]).astype(jnp.bfloat16)
    attn_out = (
        attended.reshape(kv_local, slots, per_kv, BLOCK, HD)
        .transpose(1, 3, 0, 2, 4)
        .reshape(tok_rows, kv_local * per_kv * HD)
    )
    return (mamba_out, attn_out)


def solution(mesh):
    in_specs = (
        P(("group", "seq"), "head"),
        P("head", ("group", "seq")),
        P("head"),
        P("head"),
        P(("group", "seq"), None),
        P(("group", "seq"), None),
        P(("group", "seq"), "head"),
        P(("group", "seq"), "head"),
        P(("group", "seq"), "head"),
    )
    out_specs = (P(("group", "seq"), "head"), P(("group", "seq"), "head"))
    return jax.shard_map(local, mesh=mesh, in_specs=in_specs, out_specs=out_specs, check_vma=False)
```

profile of v0, /device:TPU:0, one launch (start us, length us, event | category | flops | bytes accessed | tf_op | source)
XLA Modules:
  0.0 329.5 jit_solution(400362677163292108)
XLA Ops:
  7.2 0.7 all-gather.6.cloned.1.call-update
  8.0 0.7 all-gather.8.cloned.1.call-update
  8.7 0.7 exponential_negate_fusion
  9.4 0.8 broadcast_multiply_fusion
  10.9 3.3 %reshape.215 = bf16[2,128,32,64]{3,2,1,0:T(8,128)(2,1)S(1)} reshape(bf16[256,2048]{1,0:T(8,128)(2,1)} %param.13) | data formatting | bytes 2097152 | tf_op jit(solution)/shard_map/reshape | solution.py:78
  14.3 2.2 copy.44
  16.6 2.1 fusion.48
  18.9 22.4 %all-gather = bf16[16,32,1]{1,2,0:T(2,128)(2,1)S(1)} all-gather(bf16[2,32,1]{1,2,0:T(2,128)(2,1)S(1)} %copy.46), channel_id=2, replica_groups=mesh['group'=2,'seq'=8,'head'=2] {'seq'}, dimensions={0}, use_global_device_ids=true | all-gather | bytes 1152 | tf_op jit(solution)/shard_map/all_gather | solution.py:18
  41.4 2.2 reshape.198
  43.6 2.0 copy.50
  45.8 3.4 %fusion.24 = f32[2,32,128,64]{2,3,1,0:T(8,128)} fusion(bf16[2,128,32,64]{1,3,2,0:T(8,128)(2,1)S(1)} %copy.44, f32[2,32,128]{2,1,0:T(8,128)S(1)} %bitcast_bitcast_fusion.1, f32[2,32,128]{2,1,0:T(8,128)S(1)} %reduce_window_sum.11, f32[2,128,128]{2,1,0:T(8,128)S(1)} %fusion.49, pred[128,128]{1,0:T(8,128)(4,1)S(1)} %iota_compare_fusion), kind=kOutput, calls=%fused_computation.35 | convolution fusion | flops 139460608 | bytes 3358720 | tf_op jit(solution)/shard_map/chij,cjhp->cihp/dot_general | solution.py:49
  49.2 4.0 %all-gather.6.cloned.1.call-done = bf16[2,1024,256]{2,1,0:T(8,128)(2,1)} async-done(((bf16[2,128,256]{2,1,0:T(8,128)(2,1)}), bf16[2,1024,256]{2,1,0:T(8,128)(2,1)}) %all-gather.6.cloned.1.call-update) | async-done | bytes 1048592 | tf_op jit(solution)/shard_map/all_gather | solution.py:124
  53.1 2.2 reshape.197
  55.4 39.0 %all-gather.8.cloned.1.call-done = bf16[2,1024,256]{2,1,0:T(8,128)(2,1)} async-done(((bf16[2,128,256]{2,1,0:T(8,128)(2,1)}), bf16[2,1024,256]{2,1,0:T(8,128)(2,1)}) %all-gather.8.cloned.1.call-update) | async-done | bytes 1048592 | tf_op jit(solution)/shard_map/all_gather | solution.py:125
  94.3 2.1 reshape.201
  96.4 123.7 %all-gather.10.cloned.1.call-done = bf16[16,32,64,128]{3,2,1,0:T(8,128)(2,1)} async-done(((bf16[2,32,64,128]{3,2,1,0:T(8,128)(2,1)}), bf16[16,32,64,128]{3,2,1,0:T(8,128)(2,1)}) %all-gather.10.cloned.1.call-update) | async-done | bytes 8388624 | tf_op jit(solution)/shard_map/all_gather | solution.py:18
  220.2 14.6 %while.31 = (s32[]{:T(128)}, f32[2,32]{1,0:T(2,128)S(1)}, f32[2,32,64,128]{3,2,1,0:T(8,128)S(1)}, s32[]{:T(128)}, bf16[8,2,32]{2,1,0:T(2,128)(2,1)S(1)}, /*index...) while((s32[]{:T(128)}, f32[2,32]{1,0:T(2,128)S(1)}, f32[2,32,64,128]{3,2,1,0:T(8,128)S(1)}, ...), condition=%wide.region_2.3_spmd.clone, body=%wide.region_1.2_spmd.clone.sunk | while | flops 2621764 | bytes 5244279 | solution.py:35
  220.2 1.8 fusion.73
  222.0 1.8 fusion.73
  223.8 1.8 fusion.73
  225.6 1.8 fusion.73
  227.5 1.8 fusion.73
  229.3 1.8 fusion.73
  231.1 1.8 fusion.73
  232.9 1.8 fusion.73
  234.8 3.0 fusion.41
  237.7 41.9 %while.32 = (s32[]{:T(128)}, f32[2,1024]{1,0:T(2,128)S(1)}, f32[2,1024]{1,0:T(2,128)S(1)}, f32[2,1024,128]{2,1,0:T(8,128)}, s32[2]{0:T(128)S(1)}, /*index=5*/bf1...) while((s32[]{:T(128)}, f32[2,1024]{1,0:T(2,128)S(1)}, ...), condition=%wide.region_8.9_spmd.clone, body=%wide.region_5.8_spmd.clone.sunk | while | flops 1102851072 | bytes 83518768 | solution.py:156
  239.1 0.7 broadcast_compare_fusion.2
  239.7 2.7 constant_dynamic-slice_fusion.3
  242.6 5.0 %fusion.80 = (f32[2,1024]{1,0:T(2,128)S(1)}, f32[2,1024,1024]{2,1,0:T(8,128)}) fusion(pred[1024,1024]{0,1:T(8,128)(4,1)S(1)} %broadcast_compare_fusion.2, bf16[1024,2,128]{2,0,1:T(8,128)(2,1)S(1)} %bitcast.142, bf16[2,1024,128]{2,1,0:T(8,128)(2,1)S(1)} %copy-done.8), kind=kOutput, calls=%fused_computation.9.clone.1 | convolution fusion | flops 543160320 | bytes 10493952 | tf_op jit(solution)/shard_map/while/body/eval_jaxpr/gqd,kgd->gqk/dot_general | solution.py:142
  247.6 4.8 %fusion.82 = f32[2,1024]{1,0:T(2,128)S(1)} fusion(f32[2,1024,1024]{2,1,0:T(8,128)} %get-tuple-element.407, f32[2,1024]{1,0:T(2,128)S(1)} %fusion.81, pred[1024,1024]{0,1:T(8,128)(4,1)S(1)} %broadcast_compare_fusion.2), kind=kLoop, calls=%fused_computation.11.clone.1 | loop fusion | flops 10483712 | bytes 9453568 | tf_op jit(solution)/shard_map/while/body/eval_jaxpr/reduce_sum | solution.py:149
  252.5 1.2 copy-done.1
  254.0 3.7 %fusion.84 = f32[2,1024,128]{2,1,0:T(8,128)S(1)} fusion(bf16[1024,2,128]{2,0,1:T(8,128)(2,1)S(1)} %bitcast.141, f32[2,1024,1024]{2,1,0:T(8,128)S(1)} %copy-done.1, f32[2,1024]{1,0:T(2,128)S(1)} %fusion.81, pred[1024,1024]{0,1:T(8,128)(4,1)S(1)} %broadcast_compare_fusion.2, f32[2,1024,128]{2,1,0:T(8,128)S(1)} %copy-done.6, ...), kind=kOutput, calls=%fused_computation.15.clone.1 | convolution fusion | flops 548143104 | bytes 12075009 | tf_op jit(solution)/shard_map/while/body/eval_jaxpr/gqk,kgd->gqd/dot_general | solution.py:150
  257.7 1.0 copy-done.7
  260.7 2.8 constant_dynamic-slice_fusion.3
  263.6 5.0 %fusion.80 = (f32[2,1024]{1,0:T(2,128)S(1)}, f32[2,1024,1024]{2,1,0:T(8,128)}) fusion(pred[1024,1024]{0,1:T(8,128)(4,1)S(1)} %broadcast_compare_fusion.2, bf16[1024,2,128]{2,0,1:T(8,128)(2,1)S(1)} %bitcast.142, bf16[2,1024,128]{2,1,0:T(8,128)(2,1)S(1)} %copy-done.8), kind=kOutput, calls=%fused_computation.9.clone.1 | convolution fusion | flops 543160320 | bytes 10493952 | tf_op jit(solution)/shard_map/while/body/eval_jaxpr/gqd,kgd->gqk/dot_general | solution.py:142
  268.6 4.8 %fusion.82 = f32[2,1024]{1,0:T(2,128)S(1)} fusion(f32[2,1024,1024]{2,1,0:T(8,128)} %get-tuple-element.407, f32[2,1024]{1,0:T(2,128)S(1)} %fusion.81, pred[1024,1024]{0,1:T(8,128)(4,1)S(1)} %broadcast_compare_fusion.2), kind=kLoop, calls=%fused_computation.11.clone.1 | loop fusion | flops 10483712 | bytes 9453568 | tf_op jit(solution)/shard_map/while/body/eval_jaxpr/reduce_sum | solution.py:149
  273.6 1.2 copy-done.1
  274.9 3.7 %fusion.84 = f32[2,1024,128]{2,1,0:T(8,128)S(1)} fusion(bf16[1024,2,128]{2,0,1:T(8,128)(2,1)S(1)} %bitcast.141, f32[2,1024,1024]{2,1,0:T(8,128)S(1)} %copy-done.1, f32[2,1024]{1,0:T(2,128)S(1)} %fusion.81, pred[1024,1024]{0,1:T(8,128)(4,1)S(1)} %broadcast_compare_fusion.2, f32[2,1024,128]{2,1,0:T(8,128)S(1)} %copy-done.6, ...), kind=kOutput, calls=%fused_computation.15.clone.1 | convolution fusion | flops 548143104 | bytes 12075009 | tf_op jit(solution)/shard_map/while/body/eval_jaxpr/gqk,kgd->gqd/dot_general | solution.py:150
  278.7 1.0 copy-done.7
  279.7 1.6 divide_convert_fusion
  281.7 1.2 reshape.203
  282.9 18.6 %psum.14 = bf16[2,32]{1,0:T(2,128)(2,1)S(1)} all-reduce(bf16[2,32]{1,0:T(2,128)(2,1)S(1)} %broadcast_select_fusion.1), channel_id=1, replica_groups=mesh['group'=2,'seq'=8,'head'=2] {'seq'}, use_global_device_ids=true, to_apply=%region_3.4 | all-reduce | flops 64 | bytes 256 | tf_op jit(solution)/shard_map/psum | solution.py:40
  301.5 12.5 %all-reduce.2.cloned.1.call-done = bf16[2,32,64,128]{3,2,1,0:T(8,128)(2,1)} async-done(((bf16[2,32,64,128]{3,2,1,0:T(8,128)(2,1)}), bf16[2,32,64,128]{3,2,1,0:T(8,128)(2,1)}) %all-reduce.2.cloned.1.call-update) | async-done | bytes 1048592 | tf_op jit(solution)/shard_map/psum | solution.py:40
  314.0 1.5 slice_add_fusion.1
  316.1 1.5 fusion.27
  317.6 3.0 copy.58
  320.6 2.4 reshape.214
  (97 shorter events, 5.4 us)
Async XLA Ops:
  7.2 9.5 %copy-start = (bf16[256,128]{1,0:T(8,128)(2,1)S(1)}, bf16[256,128]{1,0:T(8,128)(2,1)}, u32[]{:S(2)}) copy-start(bf16[256,128]{1,0:T(8,128)(2,1)} %param.17) | copy-start | bytes 196612
  7.2 46.0 %all-gather.6.cloned.1.call-start = ((), (), s32[]{:S(2)}) async-start(), calls=%async_computation.1 | async-start | bytes 1179648 | tf_op jit(solution)/shard_map/all_gather | solution.py:124
  7.9 86.4 %all-gather.8.cloned.1.call-start = ((), (), s32[]{:S(2)}) async-start(), calls=%async_computation.2 | async-start | bytes 1179648 | tf_op jit(solution)/shard_map/all_gather | solution.py:125
  8.7 211.5 %all-gather.10.cloned.1.call-start = ((), (), s32[]{:S(2)}) async-start(), calls=%async_computation.3 | async-start | bytes 9437184 | tf_op jit(solution)/shard_map/all_gather | solution.py:18
  14.3 2.2 copy-start.9
  16.5 29.3 %copy-start.3 = (bf16[2,128,32,64]{1,3,2,0:T(8,128)(2,1)}, bf16[2,128,32,64]{1,3,2,0:T(8,128)(2,1)S(1)}, u32[]{:S(2)}) copy-start(bf16[2,128,32,64]{1,3,2,0:T(8,128)(2,1)S(1)} %copy.44) | copy-start | bytes 3145732
  18.8 26.9 %copy-start.10 = (bf16[256,128]{1,0:T(8,128)(2,1)S(1)}, bf16[256,128]{1,0:T(8,128)(2,1)}, u32[]{:S(2)}) copy-start(bf16[256,128]{1,0:T(8,128)(2,1)} %param.18) | copy-start | bytes 196612
  18.8 295.2 %all-reduce.2.cloned.1.call-start = ((), (), s32[]{:S(2)}) async-start(), calls=%async_computation | async-start | bytes 2097152 | tf_op jit(solution)/shard_map/psum | solution.py:40
  239.1 3.5 %copy-start.8 = (bf16[2,1024,128]{2,1,0:T(8,128)(2,1)S(1)}, bf16[2,1024,128]{2,1,0:T(8,128)(2,1)}, u32[]{:S(2)}) copy-start(bf16[2,1024,128]{2,1,0:T(8,128)(2,1)} %get-tuple-element.465) | copy-start | bytes 1572868 | tf_op jit(solution)/shard_map/while
  247.6 4.9 %copy-start.2 = (bf16[1,2,512,2,128]{4,3,2,0,1:T(2,128)(2,1)S(1)}, bf16[1,2,512,2,128]{4,3,2,0,1:T(2,128)(2,1)}, u32[]{:S(2)}) copy-start(bf16[1,2,512,2,128]{4,3,2,0,1:T(2,128)(2,1)} %get-tuple-element.409) | copy-start | bytes 1572868 | tf_op jit(solution)/shard_map/while
  247.6 6.2 %copy-start.1 = (f32[2,1024,1024]{2,1,0:T(8,128)S(1)}, f32[2,1024,1024]{2,1,0:T(8,128)}, u32[]{:S(2)}) copy-start(f32[2,1024,1024]{2,1,0:T(8,128)} %get-tuple-element.407) | copy-start | bytes 25165828 | tf_op jit(solution)/shard_map/while
  247.6 6.4 %copy-start.6 = (f32[2,1024,128]{2,1,0:T(8,128)S(1)}, f32[2,1024,128]{2,1,0:T(8,128)}, u32[]{:S(2)}) copy-start(f32[2,1024,128]{2,1,0:T(8,128)} %get-tuple-element.450) | copy-start | bytes 3145732 | tf_op jit(solution)/shard_map/while
  257.7 1.0 copy-start.7
  260.0 3.5 %copy-start.8 = (bf16[2,1024,128]{2,1,0:T(8,128)(2,1)S(1)}, bf16[2,1024,128]{2,1,0:T(8,128)(2,1)}, u32[]{:S(2)}) copy-start(bf16[2,1024,128]{2,1,0:T(8,128)(2,1)} %get-tuple-element.465) | copy-start | bytes 1572868 | tf_op jit(solution)/shard_map/while
  268.6 4.9 %copy-start.2 = (bf16[1,2,512,2,128]{4,3,2,0,1:T(2,128)(2,1)S(1)}, bf16[1,2,512,2,128]{4,3,2,0,1:T(2,128)(2,1)}, u32[]{:S(2)}) copy-start(bf16[1,2,512,2,128]{4,3,2,0,1:T(2,128)(2,1)} %get-tuple-element.409) | copy-start | bytes 1572868 | tf_op jit(solution)/shard_map/while
  268.6 6.1 %copy-start.1 = (f32[2,1024,1024]{2,1,0:T(8,128)S(1)}, f32[2,1024,1024]{2,1,0:T(8,128)}, u32[]{:S(2)}) copy-start(f32[2,1024,1024]{2,1,0:T(8,128)} %get-tuple-element.407) | copy-start | bytes 25165828 | tf_op jit(solution)/shard_map/while
  268.6 6.3 %copy-start.6 = (f32[2,1024,128]{2,1,0:T(8,128)S(1)}, f32[2,1024,128]{2,1,0:T(8,128)}, u32[]{:S(2)}) copy-start(f32[2,1024,128]{2,1,0:T(8,128)} %get-tuple-element.450) | copy-start | bytes 3145732 | tf_op jit(solution)/shard_map/while
  278.7 1.0 copy-start.7
  314.0 1.5 copy-start.4
  314.0 2.1 copy-start.5
  314.0 2.1 copy-start.11
Sparse Core Ops, SparseCore 0:
  10.2 42.9 all-gather.5
  55.3 38.9 all-gather.7
  96.4 123.6 all-gather.9
  237.8 76.1 all-reduce.1
where the time goes:
time: 330 us
  waiting for transfers between devices  181 us (55%)
  blocking collectives  41.1 us (12%)
  other arithmetic  33.8 us (10%)
  local copies, waits for them, and re-layouts  33.6 us (10%)
  matrix products  24.6 us (7%)
  between operations  14 us (4%)
    all_gather x1, waiting for transfers between devices, carried_in(): lax.all_gather(part.astype(kind), axis)  124 us
    all_gather x1, waiting for transfers between devices, local(): v_piece = lax.all_gather(v_slots, 'seq', axis=1, tiled=True)  39 us
    all_gather x1, blocking collectives, carried_in(): lax.all_gather(part.astype(kind), axis)  22.4 us
    psum x1, blocking collectives, broadcast(): return lax.psum(kept, axis)  18.6 us
    select_n x16, other arithmetic, turn(): return jax.tree.map(lambda a, b: jnp.where(reached, a, b), new, before)  14.3 us
    psum x1, waiting for transfers between devices, broadcast(): return lax.psum(kept, axis)  12.5 us
    dot_general x2, matrix products, per_block(): jnp.einsum('gqd,kgd->gqk', q_flat, k_flat, preferred_element_type=jnp.flo...  10 us
    reduce_sum x2, other arithmetic, per_block(): new_sum = run_sum * rescale + jnp.sum(weights, axis=-1)  9.6 us
  transfers between devices with their start and end apart: 4, of which 4 were waited for; matrix products, arithmetic and copies ran while one was open for 18% of the time, Pallas kernels for 0%

commit v1 on v0

--- a/solution.py
+++ b/solution.py
@@ -10,6 +10,18 @@
 KVHEADS = 4
 HD = 128
 NEG = -1e30
+
+
+def gather_by_bits(x, axis, dim):
+    ways, here, turn = (lax.axis_size(axis), lax.axis_index(axis), x.shape[dim])
+    line, have = (x, 1)
+    while have < ways:
+        line = jnp.concatenate(
+            [line, lax.ppermute(line, axis, [(d, (d - have) % ways) for d in range(ways)])],
+            axis=dim,
+        )
+        have = 2 * have
+    return jnp.roll(line, here * turn, axis=dim)
 
 
 def carried_in(value, axis, combine, identity):
@@ -122,7 +134,7 @@
     )
     running = start_state
     k_piece = lax.all_gather(k_slots, "seq", axis=1, tiled=True)
-    v_piece = lax.all_gather(v_slots, "seq", axis=1, tiled=True)
+    v_piece = gather_by_bits(v_slots, "seq", 1)
     rows = k_piece.shape[1]
     block_rows = 512
     count = rows // block_rows

time: 330 us -> 316 us (0.958)
  waiting for transfers between devices: 181 us -> 142 us
  other arithmetic: 33.8 us -> 47.7 us
  starting transfers between devices: 0.16 us -> 7.68 us
    all_gather x1 -> x0, waiting for transfers between devices: 39 us -> none  [local(): v_piece = lax.all_gather(v_slots, 'seq', axis=1, tiled=True)]
    ppermute x0 -> x3, waiting for transfers between devices: none -> 17.1 us  [gather_by_bits(): lax.ppermute(line, axis, [(d, (d - have) % ways) for d in range(ways)])]
    all_gather x1, waiting for transfers between devices: 124 us -> 111 us  [carried_in(): lax.all_gather(part.astype(kind), axis)]
    ppermute x0 -> x3, starting transfers between devices: none -> 7.57 us  [gather_by_bits(): lax.ppermute(line, axis, [(d, (d - have) % ways) for d in range(ways)])]
    convert_element_type x8, other arithmetic: 0.06 us -> 5.26 us  [turn(): part[k].astype(own.dtype)]
    select_n x16, other arithmetic: 14.3 us -> 19.5 us  [turn(): return jax.tree.map(lambda a, b: jnp.where(reached, a, b), new, before)]
    all_gather x1, waiting for transfers between devices: 3.96 us -> 0.01 us  [local(): k_piece = lax.all_gather(k_slots, 'seq', axis=1, tiled=True)]
    unnamed x18 -> x45, local copies, waits for them, and re-layouts: 6.11 us -> 7.52 us
  transfers between devices with their start and end apart: 4 -> 6, of which waited for: 4 -> 4; matrix products, arithmetic and copies ran while one was open for 18% -> 22% of each run, Pallas kernels for 0% -> 0%
where the time goes in v1:
time: 316 us; the launch traced here: 315 us
  waiting for transfers between devices  142 us (45%)
  other arithmetic  47.7 us (15%)
  blocking collectives  39.4 us (12%)
  local copies, waits for them, and re-layouts  36 us (11%)
  matrix products  26.7 us (8%)
  between operations  14 us (4%)
  starting transfers between devices  7.68 us (2%)
    all_gather x1, waiting for transfers between devices, carried_in(): lax.all_gather(part.astype(kind), axis)  111 us
    all_gather x1, blocking collectives, carried_in(): lax.all_gather(part.astype(kind), axis)  20.8 us
    select_n x16, other arithmetic, turn(): return jax.tree.map(lambda a, b: jnp.where(reached, a, b), new, before)  19.5 us
    psum x1, blocking collectives, broadcast(): return lax.psum(kept, axis)  18.6 us
    ppermute x3, waiting for transfers between devices, gather_by_bits(): lax.ppermute(line, axis, [(d, (d - have) % ways) for d in range(ways)])  17.1 us
    psum x1, waiting for transfers between devices, broadcast(): return lax.psum(kept, axis)  12.4 us
    dot_general x2, matrix products, per_block(): jnp.einsum('gqd,kgd->gqk', q_flat, k_flat, preferred_element_type=jnp.flo...  10.1 us
    reduce_sum x2, other arithmetic, per_block(): new_sum = run_sum * rescale + jnp.sum(weights, axis=-1)  9.6 us
  transfers between devices with their start and end apart: 6, of which 4 were waited for; matrix products, arithmetic and copies ran while one was open for 22% of the time, Pallas kernels for 0%

profile of v1, /device:TPU:0, one launch (start us, length us, event | category | flops | bytes accessed | tf_op | source)
XLA Modules:
  0.0 314.5 jit_solution(10342147192768384529)
XLA Ops:
  8.6 0.8 broadcast_multiply_fusion
  10.2 3.3 %reshape.215 = bf16[2,128,32,64]{3,2,1,0:T(8,128)(2,1)S(1)} reshape(bf16[256,2048]{1,0:T(8,128)(2,1)} %param.13) | data formatting | bytes 2097152 | tf_op jit(solution)/shard_map/reshape | solution.py:90
  13.6 2.2 copy.44
  15.9 2.2 fusion.48
  18.2 6.0 %collective-permute-start = (bf16[2,128,256]{2,1,0:T(8,128)(2,1)S(1)}, bf16[2,128,256]{2,1,0:T(8,128)(2,1)S(1)}, u32[]{:S(2)}, u32[]{:S(2)}) collective-permute-start(bf16[2,128,256]{2,1,0:T(8,128)(2,1)S(1)} %bitcast.149), channel_id=1, source_target_pairs={{0,14},{2,0},{4,2},{6,4},{8,6},{10,8},{12,10},{14,12},{1,15},{3,1}... | collective-permute-start | bytes 393224 | tf_op jit(solution)/shard_map/ppermute | solution.py:20
  27.3 1.1 collective-permute-done
  29.2 1.5 collective-permute-start.1
  31.3 2.2 reshape.198
  33.5 1.9 copy.50
  36.1 20.8 %all-gather = bf16[16,32,1]{1,2,0:T(2,128)(2,1)S(1)} all-gather(bf16[2,32,1]{1,2,0:T(2,128)(2,1)S(1)} %copy.46), channel_id=2, replica_groups=mesh['group'=2,'seq'=8,'head'=2] {'seq'}, dimensions={0}, use_global_device_ids=true | all-gather | bytes 1152 | tf_op jit(solution)/shard_map/all_gather | solution.py:30
  57.5 1.0 fusion.49
  58.5 1.0 pad_maximum_fusion
  59.6 4.4 %fusion.24 = f32[2,32,128,64]{2,3,1,0:T(8,128)} fusion(bf16[2,128,32,64]{1,3,2,0:T(8,128)(2,1)S(1)} %copy.44, f32[2,32,128]{2,1,0:T(8,128)} %bitcast_bitcast_fusion.1, f32[2,32,128]{2,1,0:T(8,128)S(1)} %reduce_window_sum.11, f32[2,128,128]{2,1,0:T(8,128)S(1)} %fusion.49, pred[128,128]{1,0:T(8,128)(4,1)} %iota_compare_fusion), kind=kOutput, calls=%fused_computation.35 | convolution fusion | flops 139460608 | bytes 3358720 | tf_op jit(solution)/shard_map/chij,cjhp->cihp/dot_general | solution.py:61
  64.1 15.9 %collective-permute-done.2 = bf16[2,512,256]{2,1,0:T(8,128)(2,1)S(1)} collective-permute-done((bf16[2,512,256]{2,1,0:T(8,128)(2,1)S(1)}, bf16[2,512,256]{2,1,0:T(8,128)(2,1)S(1)}, u32[]{:S(2)}, u32[]{:S(2)}) %collective-permute-start.2) | collective-permute-done | bytes 524320 | tf_op jit(solution)/shard_map/ppermute | solution.py:20
  80.3 1.1 reshape.201
  81.4 2.2 reshape.197
  83.6 111.4 %all-gather.7.cloned.1.call-done = bf16[16,32,64,128]{3,2,1,0:T(8,128)(2,1)} async-done(((bf16[2,32,64,128]{3,2,1,0:T(8,128)(2,1)}), bf16[16,32,64,128]{3,2,1,0:T(8,128)(2,1)}) %all-gather.7.cloned.1.call-update) | async-done | bytes 8388624 | tf_op jit(solution)/shard_map/all_gather | solution.py:30
  195.0 24.8 %while.31 = (s32[]{:T(128)}, f32[2,32]{1,0:T(2,128)S(1)}, f32[2,32,64,128]{3,2,1,0:T(8,128)S(1)}, s32[]{:T(128)}, bf16[8,2,32]{2,1,0:T(2,128)(2,1)}, /*index=5*/...) while((s32[]{:T(128)}, f32[2,32]{1,0:T(2,128)S(1)}, f32[2,32,64,128]{3,2,1,0:T(8,128)S(1)}, ...), condition=%wide.region_2.3_spmd.clone, body=%wide.region_1.2_spmd.clone.sunk | while | flops 2621764 | bytes 5244279 | solution.py:47
  195.6 1.8 fusion.73
  198.7 1.8 fusion.73
  201.8 1.8 fusion.73
  204.9 1.8 fusion.73
  208.0 1.8 fusion.73
  211.1 1.8 fusion.73
  214.2 1.8 fusion.73
  217.3 1.8 fusion.73
  219.8 2.9 fusion.41
  222.7 42.1 %while.32 = (s32[]{:T(128)}, f32[2,1024]{1,0:T(2,128)S(1)}, f32[2,1024]{1,0:T(2,128)S(1)}, f32[2,1024,128]{2,1,0:T(8,128)}, s32[2]{0:T(128)S(1)}, /*index=5*/bf1...) while((s32[]{:T(128)}, f32[2,1024]{1,0:T(2,128)S(1)}, ...), condition=%wide.region_8.9_spmd.clone, body=%wide.region_5.8_spmd.clone.sunk | while | flops 1102851072 | bytes 83518768 | solution.py:168
  224.7 2.7 constant_dynamic-slice_fusion.4
  227.6 5.1 %fusion.80 = (f32[2,1024]{1,0:T(2,128)S(1)}, f32[2,1024,1024]{2,1,0:T(8,128)}) fusion(pred[1024,1024]{0,1:T(8,128)(4,1)S(1)} %broadcast_compare_fusion.2, bf16[1024,2,128]{2,0,1:T(8,128)(2,1)S(1)} %bitcast.142, bf16[2,1024,128]{2,1,0:T(8,128)(2,1)S(1)} %copy-done.13), kind=kOutput, calls=%fused_computation.9.clone.1 | convolution fusion | flops 543160320 | bytes 10493952 | tf_op jit(solution)/shard_map/while/body/eval_jaxpr/gqd,kgd->gqk/dot_general | solution.py:154
  232.7 4.8 %fusion.82 = f32[2,1024]{1,0:T(2,128)S(1)} fusion(f32[2,1024,1024]{2,1,0:T(8,128)} %get-tuple-element.407, f32[2,1024]{1,0:T(2,128)S(1)} %fusion.81, pred[1024,1024]{0,1:T(8,128)(4,1)S(1)} %broadcast_compare_fusion.2), kind=kLoop, calls=%fused_computation.11.clone.1 | loop fusion | flops 10483712 | bytes 9453568 | tf_op jit(solution)/shard_map/while/body/eval_jaxpr/reduce_sum | solution.py:161
  237.6 1.2 copy-done.1
  239.0 3.7 %fusion.84 = f32[2,1024,128]{2,1,0:T(8,128)S(1)} fusion(bf16[1024,2,128]{2,0,1:T(8,128)(2,1)S(1)} %bitcast.141, f32[2,1024,1024]{2,1,0:T(8,128)S(1)} %copy-done.1, f32[2,1024]{1,0:T(2,128)S(1)} %fusion.81, pred[1024,1024]{0,1:T(8,128)(4,1)S(1)} %broadcast_compare_fusion.2, f32[2,1024,128]{2,1,0:T(8,128)S(1)} %copy-done.10, ...), kind=kOutput, calls=%fused_computation.15.clone.1 | convolution fusion | flops 548143104 | bytes 12075009 | tf_op jit(solution)/shard_map/while/body/eval_jaxpr/gqk,kgd->gqd/dot_general | solution.py:162
  242.8 1.0 copy-done.11
  245.8 2.8 constant_dynamic-slice_fusion.4
  248.7 5.1 %fusion.80 = (f32[2,1024]{1,0:T(2,128)S(1)}, f32[2,1024,1024]{2,1,0:T(8,128)}) fusion(pred[1024,1024]{0,1:T(8,128)(4,1)S(1)} %broadcast_compare_fusion.2, bf16[1024,2,128]{2,0,1:T(8,128)(2,1)S(1)} %bitcast.142, bf16[2,1024,128]{2,1,0:T(8,128)(2,1)S(1)} %copy-done.13), kind=kOutput, calls=%fused_computation.9.clone.1 | convolution fusion | flops 543160320 | bytes 10493952 | tf_op jit(solution)/shard_map/while/body/eval_jaxpr/gqd,kgd->gqk/dot_general | solution.py:154
  253.7 4.8 %fusion.82 = f32[2,1024]{1,0:T(2,128)S(1)} fusion(f32[2,1024,1024]{2,1,0:T(8,128)} %get-tuple-element.407, f32[2,1024]{1,0:T(2,128)S(1)} %fusion.81, pred[1024,1024]{0,1:T(8,128)(4,1)S(1)} %broadcast_compare_fusion.2), kind=kLoop, calls=%fused_computation.11.clone.1 | loop fusion | flops 10483712 | bytes 9453568 | tf_op jit(solution)/shard_map/while/body/eval_jaxpr/reduce_sum | solution.py:161
  258.7 1.2 copy-done.1
  260.1 3.7 %fusion.84 = f32[2,1024,128]{2,1,0:T(8,128)S(1)} fusion(bf16[1024,2,128]{2,0,1:T(8,128)(2,1)S(1)} %bitcast.141, f32[2,1024,1024]{2,1,0:T(8,128)S(1)} %copy-done.1, f32[2,1024]{1,0:T(2,128)S(1)} %fusion.81, pred[1024,1024]{0,1:T(8,128)(4,1)S(1)} %broadcast_compare_fusion.2, f32[2,1024,128]{2,1,0:T(8,128)S(1)} %copy-done.10, ...), kind=kOutput, calls=%fused_computation.15.clone.1 | convolution fusion | flops 548143104 | bytes 12075009 | tf_op jit(solution)/shard_map/while/body/eval_jaxpr/gqk,kgd->gqd/dot_general | solution.py:162
  263.8 1.0 copy-done.11
  264.8 1.6 divide_convert_fusion
  266.8 1.2 reshape.203
  268.0 18.6 %psum.14 = bf16[2,32]{1,0:T(2,128)(2,1)S(1)} all-reduce(bf16[2,32]{1,0:T(2,128)(2,1)S(1)} %broadcast_select_fusion.1), channel_id=1, replica_groups=mesh['group'=2,'seq'=8,'head'=2] {'seq'}, use_global_device_ids=true, to_apply=%region_3.4 | all-reduce | flops 64 | bytes 256 | tf_op jit(solution)/shard_map/psum | solution.py:52
  286.7 12.4 %all-reduce.2.cloned.1.call-done = bf16[2,32,64,128]{3,2,1,0:T(8,128)(2,1)} async-done(((bf16[2,32,64,128]{3,2,1,0:T(8,128)(2,1)}), bf16[2,32,64,128]{3,2,1,0:T(8,128)(2,1)}) %all-reduce.2.cloned.1.call-update) | async-done | bytes 1048592 | tf_op jit(solution)/shard_map/psum | solution.py:52
  299.0 1.5 slice_add_fusion.1
  301.1 1.5 fusion.27
  302.6 3.0 copy.58
  305.6 2.4 reshape.214
  (131 shorter events, 23.6 us)
Async XLA Ops:
  7.2 8.7 %copy-start = (bf16[256,128]{1,0:T(8,128)(2,1)S(1)}, bf16[256,128]{1,0:T(8,128)(2,1)}, u32[]{:S(2)}) copy-start(bf16[256,128]{1,0:T(8,128)(2,1)} %param.17) | copy-start | bytes 196612
  7.2 74.2 %all-gather.5.cloned.1.call-start = ((), (), s32[]{:S(2)}) async-start(), calls=%async_computation.1 | async-start | bytes 1179648 | tf_op jit(solution)/shard_map/all_gather | solution.py:136
  7.9 187.1 %all-gather.7.cloned.1.call-start = ((), (), s32[]{:S(2)}) async-start(), calls=%async_computation.2 | async-start | bytes 9437184 | tf_op jit(solution)/shard_map/all_gather | solution.py:30
  10.2 14.6 %copy-start.18 = (f32[2,32,1]{1,0,2:T(2,128)}, f32[2,32,1]{1,0,2:T(2,128)S(1)}, u32[]{:S(2)}) copy-start(f32[2,32,1]{1,0,2:T(2,128)S(1)} %copy.65) | copy-start | bytes 772
  13.5 2.2 copy-start.14
  15.8 43.9 %copy-start.3 = (bf16[2,128,32,64]{1,3,2,0:T(8,128)(2,1)}, bf16[2,128,32,64]{1,3,2,0:T(8,128)(2,1)S(1)}, u32[]{:S(2)}) copy-start(bf16[2,128,32,64]{1,3,2,0:T(8,128)(2,1)S(1)} %copy.44) | copy-start | bytes 3145732
  15.9 2.3 copy-start.6
  18.1 280.9 %all-reduce.2.cloned.1.call-start = ((), (), s32[]{:S(2)}) async-start(), calls=%async_computation | async-start | bytes 2097152 | tf_op jit(solution)/shard_map/psum | solution.py:52
  18.2 10.3 %collective-permute-start = (bf16[2,128,256]{2,1,0:T(8,128)(2,1)S(1)}, bf16[2,128,256]{2,1,0:T(8,128)(2,1)S(1)}, u32[]{:S(2)}, u32[]{:S(2)}) collective-permute-start(bf16[2,128,256]{2,1,0:T(8,128)(2,1)S(1)} %bitcast.149), channel_id=1, source_target_pairs={{0,14},{2,0},{4,2},{6,4},{8,6},{10,8},{12,10},{14,12},{1,15},{3,1}... | collective-permute-start | bytes 393224 | tf_op jit(solution)/shard_map/ppermute | solution.py:20
  28.5 2.9 copy-start.8
  29.2 29.3 %collective-permute-start.1 = (bf16[2,256,256]{2,1,0:T(8,128)(2,1)}, bf16[2,256,256]{2,1,0:T(8,128)(2,1)S(1)}, u32[]{:S(2)}, u32[]{:S(2)}) collective-permute-start(bf16[2,256,256]{2,1,0:T(8,128)(2,1)} %pad_maximum_fusion.1), channel_id=1, source_target_pairs={{0,12},{2,14},{4,0},{6,2},{8,4},{10,6},{12,8},{14,10},{1,13},{3,15... | collective-permute-start | bytes 786440 | tf_op jit(solution)/shard_map/ppermute | solution.py:20
  59.5 4.5 %copy-start.9 = (bf16[2,128,256]{2,1,0:T(8,128)(2,1)S(1)}, bf16[2,128,256]{2,1,0:T(8,128)(2,1)}, u32[]{:S(2)}) copy-start(bf16[2,128,256]{2,1,0:T(8,128)(2,1)} %copy-done.8) | copy-start | bytes 393220
  59.5 4.5 %copy-start.12 = (bf16[2,2048,256]{2,1,0:T(8,128)(2,1)S(1)}, bf16[2,2048,256]{2,1,0:T(8,128)(2,1)}, u32[]{:S(2)}) copy-start(bf16[2,2048,256]{2,1,0:T(8,128)(2,1)} %constant_dynamic-update-slice_fusion.7) | copy-start | bytes 6291460
  59.5 20.5 %copy-start.7 = (bf16[256,256]{1,0:T(8,128)(2,1)S(1)}, bf16[256,256]{1,0:T(8,128)(2,1)}, u32[]{:S(2)}) copy-start(bf16[256,256]{1,0:T(8,128)(2,1)} %param.21) | copy-start | bytes 393220
  59.6 20.5 %collective-permute-start.2 = (bf16[2,512,256]{2,1,0:T(8,128)(2,1)S(1)}, bf16[2,512,256]{2,1,0:T(8,128)(2,1)S(1)}, u32[]{:S(2)}, u32[]{:S(2)}) collective-permute-start(bf16[2,512,256]{2,1,0:T(8,128)(2,1)S(1)} %pad_maximum_fusion), channel_id=1, source_target_pairs={{0,8},{2,10},{4,12},{6,14},{8,0},{10,2},{12,4},{14,6},{1,9},{3,11}... | collective-permute-start | bytes 1572872 | tf_op jit(solution)/shard_map/ppermute | solution.py:20
  80.3 114.7 %copy-start.16 = (f32[2,32]{1,0:T(2,128)S(1)}, f32[2,32]{1,0:T(2,128)}, u32[]{:S(2)}) copy-start(f32[2,32]{1,0:T(2,128)} %custom-call) | copy-start | bytes 772
  195.0 24.8 %copy-start.20 = (f32[2,32]{1,0:T(2,128)S(1)}, f32[2,32]{1,0:T(2,128)}, u32[]{:S(2)}) copy-start(f32[2,32]{1,0:T(2,128)} %bitcast_exponential_fusion) | copy-start | bytes 772
  219.8 3.0 copy-start.17
  224.1 3.5 %copy-start.13 = (bf16[2,1024,128]{2,1,0:T(8,128)(2,1)S(1)}, bf16[2,1024,128]{2,1,0:T(8,128)(2,1)}, u32[]{:S(2)}) copy-start(bf16[2,1024,128]{2,1,0:T(8,128)(2,1)} %get-tuple-element.465) | copy-start | bytes 1572868 | tf_op jit(solution)/shard_map/while
  232.6 4.9 %copy-start.2 = (bf16[1,2,512,2,128]{4,3,2,0,1:T(2,128)(2,1)S(1)}, bf16[1,2,512,2,128]{4,3,2,0,1:T(2,128)(2,1)}, u32[]{:S(2)}) copy-start(bf16[1,2,512,2,128]{4,3,2,0,1:T(2,128)(2,1)} %get-tuple-element.409) | copy-start | bytes 1572868 | tf_op jit(solution)/shard_map/while
  232.6 6.2 %copy-start.1 = (f32[2,1024,1024]{2,1,0:T(8,128)S(1)}, f32[2,1024,1024]{2,1,0:T(8,128)}, u32[]{:S(2)}) copy-start(f32[2,1024,1024]{2,1,0:T(8,128)} %get-tuple-element.407) | copy-start | bytes 25165828 | tf_op jit(solution)/shard_map/while
  232.6 6.4 %copy-start.10 = (f32[2,1024,128]{2,1,0:T(8,128)S(1)}, f32[2,1024,128]{2,1,0:T(8,128)}, u32[]{:S(2)}) copy-start(f32[2,1024,128]{2,1,0:T(8,128)} %get-tuple-element.450) | copy-start | bytes 3145732 | tf_op jit(solution)/shard_map/while
  242.8 1.0 copy-start.11
  245.1 3.5 %copy-start.13 = (bf16[2,1024,128]{2,1,0:T(8,128)(2,1)S(1)}, bf16[2,1024,128]{2,1,0:T(8,128)(2,1)}, u32[]{:S(2)}) copy-start(bf16[2,1024,128]{2,1,0:T(8,128)(2,1)} %get-tuple-element.465) | copy-start | bytes 1572868 | tf_op jit(solution)/shard_map/while
  253.7 4.9 %copy-start.2 = (bf16[1,2,512,2,128]{4,3,2,0,1:T(2,128)(2,1)S(1)}, bf16[1,2,512,2,128]{4,3,2,0,1:T(2,128)(2,1)}, u32[]{:S(2)}) copy-start(bf16[1,2,512,2,128]{4,3,2,0,1:T(2,128)(2,1)} %get-tuple-element.409) | copy-start | bytes 1572868 | tf_op jit(solution)/shard_map/while
  253.7 6.1 %copy-start.1 = (f32[2,1024,1024]{2,1,0:T(8,128)S(1)}, f32[2,1024,1024]{2,1,0:T(8,128)}, u32[]{:S(2)}) copy-start(f32[2,1024,1024]{2,1,0:T(8,128)} %get-tuple-element.407) | copy-start | bytes 25165828 | tf_op jit(solution)/shard_map/while
  253.7 6.3 %copy-start.10 = (f32[2,1024,128]{2,1,0:T(8,128)S(1)}, f32[2,1024,128]{2,1,0:T(8,128)}, u32[]{:S(2)}) copy-start(f32[2,1024,128]{2,1,0:T(8,128)} %get-tuple-element.450) | copy-start | bytes 3145732 | tf_op jit(solution)/shard_map/while
  263.8 1.0 copy-start.11
  264.8 3.2 %copy-start.19 = (f32[2,32,1]{1,0,2:T(2,128)S(1)}, f32[2,32,1]{1,0,2:T(2,128)}, u32[]{:S(2)}) copy-start(f32[2,32,1]{1,0,2:T(2,128)} %copy-done.18) | copy-start | bytes 772
  299.0 1.5 copy-start.4
  299.0 2.1 copy-start.5
  299.0 2.1 copy-start.15
  299.0 2.1 copy-start.21
Sparse Core Ops, SparseCore 0:
  10.2 48.7 all-gather.4
  61.1 133.7 all-gather.6
  222.8 76.1 all-reduce.1
